TPU v7x, 256 devices: a whole 4x4x8 slice. The times are simulated.
256 devices in a mesh: dp: 8 (over y, x_hi), expert: 8 (over z), tensor: 4 (over x_lo, core).
Axes of the slice: x: 4 (x_hi: 2, x_lo: 2; x = x_hi * 2 + x_lo), y: 4, z: 8, core: 2. Of those that a mesh axis runs over, the one named last changes fastest.
Arguments:
- tokens: bfloat16 [4096, 2048], P(('dp', 'expert', 'tensor')), may hold values from -6 to 6
- cotangent: bfloat16 [4096, 2048], P(('dp', 'expert', 'tensor')), may hold values from -3 to 3
- routes: int32 [4096, 2], P(('dp', 'expert', 'tensor')), may hold values from 0 to 7, all different within a row; in each aligned block of 16 rows (0 to 15, 16 to 31, ...) at most 5 rows name the same one
- weight_codes: int32 [4096, 2], P(('dp', 'expert', 'tensor')), may hold values from 16 to 256
- dense_gate: bfloat16 [2048, 8192], P('expert', ('dp', 'tensor')), may hold values from -0.125 to 0.125
- dense_up: bfloat16 [2048, 8192], P('expert', ('dp', 'tensor')), may hold values from -0.125 to 0.125
- dense_down_t: bfloat16 [2048, 8192], P('expert', ('dp', 'tensor')), may hold values from -0.0625 to 0.0625
Outputs:
- mixed: bfloat16 [4096, 2048], P(('dp', 'expert', 'tensor'))
- input_grad: bfloat16 [4096, 2048], P(('dp', 'expert', 'tensor'))
- grad_gate: bfloat16 [8, 2048, 8192], P('expert', None, ('dp', 'tensor'))
- grad_up: bfloat16 [8, 2048, 8192], P('expert', None, ('dp', 'tensor'))
- grad_down_t: bfloat16 [8, 2048, 8192], P('expert', None, ('dp', 'tensor'))
Inputs may be any that keep to these rules, and one draw needn't show every extreme that they name: `routes`: each row names two different experts; the rows of one device name each expert at most 5 times.
All inputs are finite; a program needn't handle non-finite values.
Results may differ from a plain program's by a relative error of at most 0.02.
Values may be sent and summed in bfloat16 or wider, within the bound.
No kernel may reach another device: no remote copies, remote signals or barrier semaphores. Data moves between devices by JAX's collectives and lax.ppermute only.
A program may use at most 128 MiB of HBM per device.

v0:
```python
import jax
import jax.numpy as jnp
from jax import lax
from jax.sharding import PartitionSpec as P

GROUP = ("dp", "tensor")


def silu_parts(gate_pre):
    sigmoid_val = jax.nn.sigmoid(gate_pre)
    return (gate_pre * sigmoid_val, sigmoid_val * (1.0 + gate_pre * (1.0 - sigmoid_val)))


def contract_rows(left_side, right_side):
    return lax.dot_general(
        left_side, right_side, (((0,), (0,)), ((), ())), preferred_element_type=jnp.float32
    )


def contract_cols(left_side, right_side):
    return lax.dot_general(
        left_side, right_side, (((1,), (1,)), ((), ())), preferred_element_type=jnp.float32
    )


def forward_parts(rows_x, gate_cols, up_cols):
    gate_pre = jnp.dot(rows_x, gate_cols, preferred_element_type=jnp.float32)
    up_pre = jnp.dot(rows_x, up_cols, preferred_element_type=jnp.float32)
    activation, act_slope = silu_parts(gate_pre)
    hidden = (activation * up_pre).astype(jnp.bfloat16)
    return (up_pre, activation, act_slope, hidden)


def grad_parts(scaled, down_cols, up_pre, activation, act_slope):
    hidden_grad = jnp.dot(scaled, down_cols, preferred_element_type=jnp.float32)
    gate_grad = (hidden_grad * up_pre * act_slope).astype(jnp.bfloat16)
    up_grad = (hidden_grad * activation).astype(jnp.bfloat16)
    return (gate_grad, up_grad)


def shards(tokens, cotangent, routes, weight_codes, dense_gate, dense_up, dense_down_t):
    experts = lax.axis_size("expert")
    count_tok, model_width = tokens.shape
    hid = dense_gate.shape[1]
    capacity = 5 * count_tok // (2 * experts)
    slots_here = experts * capacity
    stacked = jnp.concatenate([dense_gate, dense_up, dense_down_t], axis=1)
    full_cols = lax.all_gather(stacked, "expert", axis=0, tiled=True)
    gate_cols = full_cols[:, :hid]
    up_cols = full_cols[:, hid : 2 * hid]
    down_cols = full_cols[:, 2 * hid :]
    gate_up_cols = full_cols[:, : 2 * hid]
    code_cols = jnp.zeros((count_tok, 128), jnp.bfloat16)
    code_cols = code_cols.at[:, 0:2].set(weight_codes.astype(jnp.bfloat16))
    home = jnp.concatenate([tokens, cotangent, code_cols], axis=1)
    plane = lax.all_gather(home, GROUP, axis=0, tiled=True)
    plane_x = plane[:, :model_width]
    plane_dy = plane[:, model_width : 2 * model_width].astype(jnp.float32)
    plane_scale = plane[:, 2 * model_width : 2 * model_width + 2].astype(jnp.float32) / 256.0
    up_pre, activation, act_slope, hidden = forward_parts(plane_x, gate_cols, up_cols)
    out_term = contract_cols(hidden, down_cols).astype(jnp.bfloat16)
    grad_term = jnp.zeros(out_term.shape, jnp.float32)
    for which in range(2):
        scaled = (plane_scale[:, which : which + 1] * plane_dy).astype(jnp.bfloat16)
        gate_grad, up_grad = grad_parts(scaled, down_cols, up_pre, activation, act_slope)
        grad_term = grad_term + contract_cols(
            jnp.concatenate([gate_grad, up_grad], axis=1), gate_up_cols
        )
    terms = jnp.concatenate([out_term, grad_term.astype(jnp.bfloat16)], axis=1)
    summed = lax.psum_scatter(terms, GROUP, scatter_dimension=0, tiled=True)
    expert_out = summed[:, :model_width].astype(jnp.float32)
    code_scale = weight_codes.astype(jnp.float32) / 256.0
    mixed = (code_scale[:, 0:1] * expert_out + code_scale[:, 1:2] * expert_out).astype(jnp.bfloat16)
    input_grad = summed[:, model_width:]
    flat_route = routes.reshape(-1)
    flat_scale = weight_codes.reshape(-1).astype(jnp.float32) / 256.0
    onehot = (flat_route[:, None] == jnp.arange(experts, dtype=jnp.int32)[None, :]).astype(
        jnp.int32
    )
    earlier = jnp.cumsum(onehot, axis=0) - onehot
    slot_of = flat_route * capacity + jnp.sum(earlier * onehot, axis=1)
    placed = (slot_of[None, :] == jnp.arange(slots_here, dtype=jnp.int32)[:, None]).astype(
        jnp.bfloat16
    )
    flat_x = jnp.repeat(tokens, 2, axis=0)
    flat_scaled = (
        flat_scale[:, None] * jnp.repeat(cotangent, 2, axis=0).astype(jnp.float32)
    ).astype(jnp.bfloat16)
    send_x = jnp.dot(placed, flat_x, preferred_element_type=jnp.float32).astype(jnp.bfloat16)
    send_s = jnp.dot(placed, flat_scaled, preferred_element_type=jnp.float32).astype(jnp.bfloat16)
    send = jnp.stack(
        [
            send_x.reshape(experts, capacity, model_width),
            send_s.reshape(experts, capacity, model_width),
        ],
        axis=1,
    )
    got = lax.all_to_all(send, "expert", split_axis=0, concat_axis=0, tiled=True)
    got = jnp.transpose(got, (1, 0, 2, 3))
    rows = lax.all_gather(got, GROUP, axis=1, tiled=True)
    rows_x = rows[0].reshape(-1, model_width)
    rows_s = rows[1].reshape(-1, model_width)
    r_up, r_act, r_slope, r_hidden = forward_parts(rows_x, gate_cols, up_cols)
    r_gate, r_upg = grad_parts(rows_s, down_cols, r_up, r_act, r_slope)
    grad_gate = contract_rows(rows_x, r_gate).astype(jnp.bfloat16)[None]
    grad_up = contract_rows(rows_x, r_upg).astype(jnp.bfloat16)[None]
    grad_down_t = contract_rows(rows_s, r_hidden).astype(jnp.bfloat16)[None]
    return (mixed, input_grad, grad_gate, grad_up, grad_down_t)


def solution(mesh):
    rows = P(("dp", "expert", "tensor"), None)
    weights = P("expert", ("dp", "tensor"))
    grads = P("expert", None, ("dp", "tensor"))
    return jax.shard_map(
        shards,
        mesh=mesh,
        in_specs=(rows, rows, rows, rows, weights, weights, weights),
        out_specs=(rows, rows, grads, grads, grads),
        check_vma=False,
    )
```

profile of v0, /device:TPU:1, one launch (start us, length us, event | category | flops | bytes accessed | tf_op | source)
XLA Modules:
  0.0 376.8 jit_solution(17290189949668021922)
XLA Ops:
  7.9 1.3 broadcast_select_fusion
  9.3 1.5 fusion.43
  10.9 1.8 pad_maximum_fusion.2
  12.8 54.0 %all-gather.4.cloned.1.call-done = bf16[512,4224]{1,0:T(8,128)(2,1)} async-done(((bf16[16,4224]{1,0:T(8,128)(2,1)}), bf16[512,4224]{1,0:T(8,128)(2,1)}) %all-gather.4.cloned.1.call-update) | async-done | bytes 4325392 | tf_op jit(solution)/shard_map/all_gather | solution.py:56
  68.0 44.9 %all-gather.6.cloned.1.call-done = bf16[2048,768]{1,0:T(8,128)(2,1)} async-done(((bf16[256,768]{1,0:T(8,128)(2,1)}), bf16[2048,768]{1,0:T(8,128)(2,1)}) %all-gather.6.cloned.1.call-update) | async-done | bytes 3145744 | tf_op jit(solution)/shard_map/all_gather | solution.py:48
  112.9 2.8 fusion.16
  115.8 2.5 fusion.18
  123.9 2.6 pad_maximum_fusion
  128.9 1.9 convolution_convert_fusion.4
  134.3 1.7 stack_reshape.6
  137.4 15.5 %all_to_all.5 = bf16[8,2,5,2048]{3,1,2,0:T(2,128)(2,1)} all-to-all(bf16[8,2,5,2048]{3,1,2,0:T(2,128)(2,1)S(1)} %copy.25), channel_id=1, replica_groups=mesh['dp'=8,'expert'=8,'tensor'=4] {'expert'}, dimensions={0} | all-to-all | bytes 655360 | tf_op jit(solution)/shard_map/all_to_all | solution.py:98
  152.9 60.5 %reduce-scatter.2.cloned.1.call-done = bf16[16,4096]{1,0:T(8,128)(2,1)} async-done(((bf16[512,4096]{1,0:T(8,128)(2,1)}), bf16[16,4096]{1,0:T(8,128)(2,1)}) %reduce-scatter.2.cloned.1.call-update) | async-done | bytes 131088 | tf_op jit(solution)/shard_map/reduce_scatter | solution.py:70
  213.4 1.5 slice.86
  214.9 1.5 multiply_convert_fusion.14
  216.5 64.0 %all-gather.8.cloned.1.call-done = bf16[2,256,5,2048]{3,0,2,1:T(2,128)(2,1)} async-done(((bf16[2,8,5,2048]{3,0,2,1:T(2,128)(2,1)}), bf16[2,256,5,2048]{3,0,2,1:T(2,128)(2,1)}) %all-gather.8.cloned.1.call-update) | async-done | bytes 10485776 | tf_op jit(solution)/shard_map/all_gather | solution.py:100
  280.5 53.6 %slice_reduce_fusion = (bf16[256,5,2048]{2,1,0:T(8,128)(2,1)}, bf16[256,5,2048]{2,1,0:T(8,128)(2,1)}) fusion(bf16[2,256,5,2048]{3,0,2,1:T(2,128)(2,1)} %all-gather.8.cloned.1.call-done), kind=kLoop, calls=%fused_computation | loop fusion | bytes 20971520 | tf_op jit(solution)/shard_map/slice | solution.py:102
  334.1 10.0 %reshape_squeeze.6 = bf16[1280,2048]{1,0:T(8,128)(2,1)} reshape(bf16[256,5,2048]{2,1,0:T(8,128)(2,1)} %get-tuple-element.18) | data formatting | bytes 10485760 | tf_op jit(solution)/shard_map/reshape;squeeze | solution.py:101
  344.2 10.0 %reshape_squeeze.7 = bf16[1280,2048]{1,0:T(8,128)(2,1)} reshape(bf16[256,5,2048]{2,1,0:T(8,128)(2,1)} %get-tuple-element.17) | data formatting | bytes 10485760 | tf_op jit(solution)/shard_map/reshape;squeeze | solution.py:102
  354.2 4.2 %fusion.24 = f32[1280,256]{1,0:T(8,128)S(1)} fusion(bf16[1280,2048]{1,0:T(8,128)(2,1)} %reshape_squeeze.6, bf16[2048,768]{1,0:T(8,128)(2,1)S(1)} %copy-done.1), kind=kOutput, calls=%fused_computation.38 | convolution fusion | flops 1342177280 | bytes 7602176 | tf_op jit(solution)/shard_map/dot_general | solution.py:27
  358.4 1.6 fusion.21
  360.0 2.9 fusion.4
  362.8 1.6 fusion.27
  364.4 2.9 fusion.3
  367.3 3.0 fusion.2
  (54 shorter events, 15.2 us)
Async XLA Ops:
  7.2 59.6 %all-gather.4.cloned.1.call-start = ((), (), s32[]{:S(2)}) async-start(), calls=%async_computation.2 | async-start | bytes 4460544 | tf_op jit(solution)/shard_map/all_gather | solution.py:56
  10.8 102.1 %all-gather.6.cloned.1.call-start = ((), (), s32[]{:S(2)}) async-start(), calls=%async_computation.3 | async-start | bytes 3538944 | tf_op jit(solution)/shard_map/all_gather | solution.py:48
  12.7 200.7 %reduce-scatter.2.cloned.1.call-start = ((), (), s32[]{:S(2)}) async-start(), calls=%async_computation.4 | async-start | bytes 4325376 | tf_op jit(solution)/shard_map/reduce_scatter | solution.py:70
  112.9 2.9 copy-start.1
  115.8 2.9 copy-start.5
  126.5 0.7 copy-start.6
  126.5 0.9 copy-start.4
  126.5 1.0 copy-start.2
  126.5 5.2 %copy-start.3 = (bf16[16,2048]{1,0:T(8,128)(2,1)S(1)}, bf16[16,2048]{1,0:T(8,128)(2,1)}, u32[]{:S(2)}) copy-start(bf16[16,2048]{1,0:T(8,128)(2,1)} %param.9) | copy-start | bytes 196612
  126.5 154.0 %all-gather.8.cloned.1.call-start = ((), (), s32[]{:S(2)}) async-start(), calls=%async_computation.5 | async-start | bytes 10813440 | tf_op jit(solution)/shard_map/all_gather | solution.py:100
  354.2 4.2 %copy-start = (bf16[1280,2048]{1,0:T(8,128)(2,1)S(1)}, bf16[1280,2048]{1,0:T(8,128)(2,1)}, u32[]{:S(2)}) copy-start(bf16[1280,2048]{1,0:T(8,128)(2,1)} %reshape_squeeze.6) | copy-start | bytes 15728644
  354.2 5.8 %slice-start = ((s8[5242880]{0:T(1024)(128)(4,1)}), s8[4194304]{0:T(1024)(128)(4,1)S(1)}, s32[]{:S(2)}) async-start(s8[5242880]{0:T(1024)(128)(4,1)} %bitcast.16), calls=%async_computation.6 | async-start | bytes 8388608
  358.4 1.6 slice-start.1
Sparse Core Ops, SparseCore 0:
  11.2 55.5 all-gather.3
  69.1 43.7 all-gather.5
  126.7 86.7 reduce-scatter.1
  216.2 64.2 all-gather.7
where the time goes:
time: 378 us; the launch traced here: 377 us
  waiting for transfers between devices  224 us (59%)
  local copies, waits for them, and re-layouts  82.6 us (22%)
  matrix products  29.2 us (8%)
  blocking collectives  15.5 us (4%)
  between operations  14 us (4%)
  other arithmetic  11.7 us (3%)
    all_gather x1, waiting for transfers between devices, shards(): rows = lax.all_gather(got, GROUP, axis=1, tiled=True)  64 us
    reduce_scatter x1, waiting for transfers between devices, shards(): summed = lax.psum_scatter(terms, GROUP, scatter_dimension=0, tiled=True)  60.5 us
    all_gather x1, waiting for transfers between devices, shards(): plane = lax.all_gather(home, GROUP, axis=0, tiled=True)  54 us
    slice x1, local copies, waits for them, and re-layouts, shards(): rows_s = rows[1].reshape(-1, model_width)  53.6 us
    all_gather x1, waiting for transfers between devices, shards(): full_cols = lax.all_gather(stacked, 'expert', axis=0, tiled=True)  44.9 us
    all_to_all x1, blocking collectives, shards(): lax.all_to_all(send, 'expert', split_axis=0, concat_axis=0, tiled=True)  15.5 us
    another operation x1, local copies, waits for them, and re-layouts, shards(): rows_x = rows[0].reshape(-1, model_width)  10 us
    another operation x1, local copies, waits for them, and re-layouts, shards(): rows_s = rows[1].reshape(-1, model_width)  10 us
  transfers between devices with their start and end apart: 4, of which 4 were waited for; matrix products, arithmetic and copies ran while one was open for 4% of the time, Pallas kernels for 0%

commit v1 on v0

--- a/solution.py
+++ b/solution.py
@@ -4,6 +4,24 @@
 from jax.sharding import PartitionSpec as P
 
 GROUP = ("dp", "tensor")
+
+
+def ring_gather(value, axis, dim):
+    ways, here, turn = (lax.axis_size(axis), lax.axis_index(axis), value.shape[dim])
+    shape = [n * ways if d == dim else n for d, n in enumerate(value.shape)]
+    full = lax.dynamic_update_slice_in_dim(
+        jnp.zeros(shape, value.dtype), value, here * turn, axis=dim
+    )
+    going_up = going_down = value
+    for far in range(1, ways // 2 + 1):
+        going_up = lax.ppermute(going_up, axis, [(d, (d + 1) % ways) for d in range(ways)])
+        full = lax.dynamic_update_slice_in_dim(full, going_up, (here - far) % ways * turn, axis=dim)
+        if 2 * far < ways:
+            going_down = lax.ppermute(going_down, axis, [(d, (d - 1) % ways) for d in range(ways)])
+            full = lax.dynamic_update_slice_in_dim(
+                full, going_down, (here + far) % ways * turn, axis=dim
+            )
+    return full
 
 
 def silu_parts(gate_pre):
@@ -45,7 +63,7 @@
     capacity = 5 * count_tok // (2 * experts)
     slots_here = experts * capacity
     stacked = jnp.concatenate([dense_gate, dense_up, dense_down_t], axis=1)
-    full_cols = lax.all_gather(stacked, "expert", axis=0, tiled=True)
+    full_cols = ring_gather(stacked, "expert", 0)
     gate_cols = full_cols[:, :hid]
     up_cols = full_cols[:, hid : 2 * hid]
     down_cols = full_cols[:, 2 * hid :]

time: 378 us -> 338 us (0.89)
  waiting for transfers between devices: 224 us -> 154 us
  starting transfers between devices: 0.16 us -> 11.4 us
  local copies, waits for them, and re-layouts: 82.6 us -> 91.9 us
  matrix products: 29.2 us -> 34.4 us
  blocking collectives: 15.5 us -> 19.4 us
    all_gather x1, waiting for transfers between devices: 54 us -> 8.1 us  [shards(): plane = lax.all_gather(home, GROUP, axis=0, tiled=True)]
    all_gather x1 -> x0, waiting for transfers between devices: 44.9 us -> none  [shards(): full_cols = lax.all_gather(stacked, 'expert', axis=0, tiled=True)]
    ppermute x0 -> x7, waiting for transfers between devices: none -> 27.7 us  [the longest x4 27.7 us: ring_gather(): lax.ppermute(going_up, axis, [(d, (d + 1) % ways) for d in range(ways)])]
    ppermute x0 -> x7, starting transfers between devices: none -> 11.3 us  [the longest x3 8.72 us: ring_gather(): lax.ppermute(going_down, axis, [(d, (d - 1) % ways) for d in range(ways)])]
    reduce_scatter x1, waiting for transfers between devices: 60.5 us -> 54.4 us  [shards(): summed = lax.psum_scatter(terms, GROUP, scatter_dimension=0, tiled=True)]
    dynamic_update_slice x0 -> x8, local copies, waits for them, and re-layouts: none -> 4.29 us  [the longest x4 2.17 us: ring_gather(): lax.dynamic_update_slice_in_dim(full, going_up, (here - far) % ways * tur...]
    all_to_all x1, blocking collectives: 15.5 us -> 19.4 us  [shards(): lax.all_to_all(send, 'expert', split_axis=0, concat_axis=0, tiled=True)]
  transfers between devices with their start and end apart: 4 -> 10, of which waited for: 4 -> 7; matrix products, arithmetic and copies ran while one was open for 4% -> 7% of each run, Pallas kernels for 0% -> 0%
where the time goes in v1:
time: 338 us; the launch traced here: 337 us
  waiting for transfers between devices  154 us (46%)
  local copies, waits for them, and re-layouts  91.9 us (27%)
  matrix products  34.4 us (10%)
  blocking collectives  19.4 us (6%)
  between operations  14 us (4%)
  starting transfers between devices  11.4 us (3%)
  other arithmetic  11.4 us (3%)
    all_gather x1, waiting for transfers between devices, shards(): rows = lax.all_gather(got, GROUP, axis=1, tiled=True)  64.2 us
    reduce_scatter x1, waiting for transfers between devices, shards(): summed = lax.psum_scatter(terms, GROUP, scatter_dimension=0, tiled=True)  54.4 us
    slice x1, local copies, waits for them, and re-layouts, shards(): rows_s = rows[1].reshape(-1, model_width)  53.6 us
    ppermute x4, waiting for transfers between devices, ring_gather(): lax.ppermute(going_up, axis, [(d, (d + 1) % ways) for d in range(ways)])  27.7 us
    all_to_all x1, blocking collectives, shards(): lax.all_to_all(send, 'expert', split_axis=0, concat_axis=0, tiled=True)  19.4 us
    dot_general x3, matrix products, contract_rows(): lax.dot_general(left_side, right_side, (((0,), (0,)), ((), ())), preferre...  11.2 us
    another operation x1, local copies, waits for them, and re-layouts, shards(): rows_s = rows[1].reshape(-1, model_width)  10 us
    another operation x1, local copies, waits for them, and re-layouts, shards(): rows_x = rows[0].reshape(-1, model_width)  10 us
  transfers between devices with their start and end apart: 10, of which 7 were waited for; matrix products, arithmetic and copies ran while one was open for 7% of the time, Pallas kernels for 0%

profile of v1, /device:TPU:1, one launch (start us, length us, event | category | flops | bytes accessed | tf_op | source)
XLA Modules:
  0.0 337.0 jit_solution(12024688188019249340)
XLA Ops:
  13.6 2.5 collective-permute-start
  16.2 4.0 %collective-permute-start.1 = (bf16[256,768]{1,0:T(8,128)(2,1)S(1)}, bf16[256,768]{1,0:T(8,128)(2,1)}, u32[]{:S(2)}, u32[]{:S(2)}) collective-permute-start(bf16[256,768]{1,0:T(8,128)(2,1)S(1)} %constant_dynamic-update-slice_fusion), channel_id=1, source_target_pairs={{0,28},{4,0},{8,4},{12,8},{16,12},{20,16},{24,20},{28,24},{1,29},{... | collective-permute-start | bytes 1179656 | tf_op jit(solution)/shard_map/ppermute | solution.py:20
  20.2 8.8 %collective-permute-done = bf16[256,768]{1,0:T(8,128)(2,1)S(1)} collective-permute-done((bf16[256,768]{1,0:T(8,128)(2,1)S(1)}, bf16[256,768]{1,0:T(8,128)(2,1)S(1)}, u32[]{:S(2)}, u32[]{:S(2)}) %collective-permute-start) | collective-permute-done | bytes 393248 | tf_op jit(solution)/shard_map/ppermute | solution.py:17
  29.7 1.9 collective-permute-start.3
  31.7 8.0 %collective-permute-done.2 = bf16[256,768]{1,0:T(8,128)(2,1)} collective-permute-done((bf16[256,768]{1,0:T(8,128)(2,1)S(1)}, bf16[256,768]{1,0:T(8,128)(2,1)}, u32[]{:S(2)}, u32[]{:S(2)}) %collective-permute-start.2) | collective-permute-done | bytes 393248 | tf_op jit(solution)/shard_map/ppermute | solution.py:17
  40.7 2.7 collective-permute-start.5
  44.5 5.2 %collective-permute-done.4 = bf16[256,768]{1,0:T(8,128)(2,1)} collective-permute-done((bf16[256,768]{1,0:T(8,128)(2,1)}, bf16[256,768]{1,0:T(8,128)(2,1)}, u32[]{:S(2)}, u32[]{:S(2)}) %collective-permute-start.4) | collective-permute-done | bytes 393248 | tf_op jit(solution)/shard_map/ppermute | solution.py:17
  52.9 5.8 %collective-permute-done.6 = bf16[256,768]{1,0:T(8,128)(2,1)S(1)} collective-permute-done((bf16[256,768]{1,0:T(8,128)(2,1)}, bf16[256,768]{1,0:T(8,128)(2,1)S(1)}, u32[]{:S(2)}, u32[]{:S(2)}) %collective-permute-start.6) | collective-permute-done | bytes 393248 | tf_op jit(solution)/shard_map/ppermute | solution.py:17
  58.6 8.1 %all-gather.3.cloned.1.call-done = bf16[512,4224]{1,0:T(8,128)(2,1)} async-done(((bf16[16,4224]{1,0:T(8,128)(2,1)}), bf16[512,4224]{1,0:T(8,128)(2,1)}) %all-gather.3.cloned.1.call-update) | async-done | bytes 4325392 | tf_op jit(solution)/shard_map/all_gather | solution.py:74
  68.1 2.3 fusion.16
  76.6 2.5 pad_maximum_fusion
  83.8 1.9 convolution_convert_fusion.4
  92.4 19.4 %all_to_all.5 = bf16[8,2,5,2048]{3,1,2,0:T(2,128)(2,1)} all-to-all(bf16[8,2,5,2048]{3,1,2,0:T(2,128)(2,1)S(1)} %copy.25), channel_id=1, replica_groups=mesh['dp'=8,'expert'=8,'tensor'=4] {'expert'}, dimensions={0} | all-to-all | bytes 655360 | tf_op jit(solution)/shard_map/all_to_all | solution.py:116
  111.8 54.4 %reduce-scatter.2.cloned.1.call-done = bf16[16,4096]{1,0:T(8,128)(2,1)} async-done(((bf16[512,4096]{1,0:T(8,128)(2,1)}), bf16[16,4096]{1,0:T(8,128)(2,1)}) %reduce-scatter.2.cloned.1.call-update) | async-done | bytes 131088 | tf_op jit(solution)/shard_map/reduce_scatter | solution.py:88
  169.3 64.2 %all-gather.5.cloned.1.call-done = bf16[2,256,5,2048]{3,0,2,1:T(2,128)(2,1)} async-done(((bf16[2,8,5,2048]{3,0,2,1:T(2,128)(2,1)}), bf16[2,256,5,2048]{3,0,2,1:T(2,128)(2,1)}) %all-gather.5.cloned.1.call-update) | async-done | bytes 10485776 | tf_op jit(solution)/shard_map/all_gather | solution.py:118
  233.5 53.6 %slice_reduce_fusion = (bf16[256,5,2048]{2,1,0:T(8,128)(2,1)}, bf16[256,5,2048]{2,1,0:T(8,128)(2,1)}) fusion(bf16[2,256,5,2048]{3,0,2,1:T(2,128)(2,1)} %all-gather.5.cloned.1.call-done), kind=kLoop, calls=%fused_computation | loop fusion | bytes 20971520 | tf_op jit(solution)/shard_map/slice | solution.py:120
  287.1 10.0 %reshape_squeeze.6 = bf16[1280,2048]{1,0:T(8,128)(2,1)} reshape(bf16[256,5,2048]{2,1,0:T(8,128)(2,1)} %get-tuple-element.18) | data formatting | bytes 10485760 | tf_op jit(solution)/shard_map/reshape;squeeze | solution.py:119
  297.1 5.2 %fusion.21 = f32[1280,256]{1,0:T(8,128)} fusion(bf16[1280,2048]{1,0:T(8,128)(2,1)} %reshape_squeeze.6, bf16[2048,768]{1,0:T(8,128)(2,1)S(1)} %constant_dynamic-update-slice_fusion.3), kind=kOutput, calls=%fused_computation.35 | convolution fusion | flops 1342177280 | bytes 7602176 | tf_op jit(solution)/shard_map/dot_general | solution.py:46
  302.3 2.6 fusion.24
  304.9 10.0 %reshape_squeeze.7 = bf16[1280,2048]{1,0:T(8,128)(2,1)} reshape(bf16[256,5,2048]{2,1,0:T(8,128)(2,1)} %get-tuple-element.17) | data formatting | bytes 10485760 | tf_op jit(solution)/shard_map/reshape;squeeze | solution.py:120
  315.0 4.2 %fusion.27 = f32[1280,256]{1,0:T(8,128)S(1)} fusion(bf16[1280,2048]{1,0:T(8,128)(2,1)} %reshape_squeeze.7, bf16[2048,768]{1,0:T(8,128)(2,1)S(1)} %constant_dynamic-update-slice_fusion.3), kind=kOutput, calls=%fused_computation.41 | convolution fusion | flops 1342177280 | bytes 7602176 | tf_op jit(solution)/shard_map/dot_general | solution.py:53
  319.2 5.4 %fusion.4 = bf16[1,2048,256]{2,1,0:T(8,128)(2,1)} fusion(bf16[1280,2048]{1,0:T(8,128)(2,1)} %reshape_squeeze.7, f32[1280,256]{1,0:T(8,128)S(1)} %copy-done.11, f32[1280,256]{1,0:T(8,128)S(1)} %copy-done.12), kind=kOutput, calls=%fused_computation.14 | convolution fusion | flops 1344667648 | bytes 8912896 | tf_op jit(solution)/shard_map/dot_general | solution.py:33
  324.6 2.9 fusion.3
  327.5 3.0 fusion.2
  (88 shorter events, 34.2 us)
Async XLA Ops:
  7.2 59.6 %all-gather.3.cloned.1.call-start = ((), (), s32[]{:S(2)}) async-start(), calls=%async_computation.2 | async-start | bytes 4460544 | tf_op jit(solution)/shard_map/all_gather | solution.py:74
  10.8 155.4 %reduce-scatter.2.cloned.1.call-start = ((), (), s32[]{:S(2)}) async-start(), calls=%async_computation.3 | async-start | bytes 4325376 | tf_op jit(solution)/shard_map/reduce_scatter | solution.py:88
  13.6 15.3 %collective-permute-start = (bf16[256,768]{1,0:T(8,128)(2,1)S(1)}, bf16[256,768]{1,0:T(8,128)(2,1)S(1)}, u32[]{:S(2)}, u32[]{:S(2)}) collective-permute-start(bf16[256,768]{1,0:T(8,128)(2,1)S(1)} %constant_dynamic-update-slice_fusion), channel_id=1, source_target_pairs={{0,4},{4,8},{8,12},{12,16},{16,20},{20,24},{24,28},{28,0},{1,5},{5... | collective-permute-start | bytes 1179656 | tf_op jit(solution)/shard_map/ppermute | solution.py:17
  16.2 12.8 %collective-permute-start.1 = (bf16[256,768]{1,0:T(8,128)(2,1)S(1)}, bf16[256,768]{1,0:T(8,128)(2,1)}, u32[]{:S(2)}, u32[]{:S(2)}) collective-permute-start(bf16[256,768]{1,0:T(8,128)(2,1)S(1)} %constant_dynamic-update-slice_fusion), channel_id=1, source_target_pairs={{0,28},{4,0},{8,4},{12,8},{16,12},{20,16},{24,20},{28,24},{1,29},{... | collective-permute-start | bytes 1179656 | tf_op jit(solution)/shard_map/ppermute | solution.py:20
  29.0 0.7 copy-start.1
  29.0 10.7 %collective-permute-start.2 = (bf16[256,768]{1,0:T(8,128)(2,1)S(1)}, bf16[256,768]{1,0:T(8,128)(2,1)}, u32[]{:S(2)}, u32[]{:S(2)}) collective-permute-start(bf16[256,768]{1,0:T(8,128)(2,1)S(1)} %collective-permute-done), channel_id=1, source_target_pairs={{0,4},{4,8},{8,12},{12,16},{16,20},{20,24},{24,28},{28,0},{1,5},{5... | collective-permute-start | bytes 1179656 | tf_op jit(solution)/shard_map/ppermute | solution.py:17
  29.7 11.0 %collective-permute-start.3 = (bf16[256,768]{1,0:T(8,128)(2,1)}, bf16[256,768]{1,0:T(8,128)(2,1)}, u32[]{:S(2)}, u32[]{:S(2)}) collective-permute-start(bf16[256,768]{1,0:T(8,128)(2,1)} %collective-permute-done.1), channel_id=1, source_target_pairs={{0,28},{4,0},{8,4},{12,8},{16,12},{20,16},{24,20},{28,24},{1,29},{... | collective-permute-start | bytes 1179656 | tf_op jit(solution)/shard_map/ppermute | solution.py:20
  39.7 10.0 %collective-permute-start.4 = (bf16[256,768]{1,0:T(8,128)(2,1)}, bf16[256,768]{1,0:T(8,128)(2,1)}, u32[]{:S(2)}, u32[]{:S(2)}) collective-permute-start(bf16[256,768]{1,0:T(8,128)(2,1)} %collective-permute-done.2), channel_id=1, source_target_pairs={{0,4},{4,8},{8,12},{12,16},{16,20},{20,24},{24,28},{28,0},{1,5},{5... | collective-permute-start | bytes 1179656 | tf_op jit(solution)/shard_map/ppermute | solution.py:17
  39.7 1.0 copy-start.2
  40.7 12.1 %collective-permute-start.5 = (bf16[256,768]{1,0:T(8,128)(2,1)}, bf16[256,768]{1,0:T(8,128)(2,1)S(1)}, u32[]{:S(2)}, u32[]{:S(2)}) collective-permute-start(bf16[256,768]{1,0:T(8,128)(2,1)} %collective-permute-done.3), channel_id=1, source_target_pairs={{0,28},{4,0},{8,4},{12,8},{16,12},{20,16},{24,20},{28,24},{1,29},{... | collective-permute-start | bytes 1179656 | tf_op jit(solution)/shard_map/ppermute | solution.py:20
  49.7 9.0 %collective-permute-start.6 = (bf16[256,768]{1,0:T(8,128)(2,1)}, bf16[256,768]{1,0:T(8,128)(2,1)S(1)}, u32[]{:S(2)}, u32[]{:S(2)}) collective-permute-start(bf16[256,768]{1,0:T(8,128)(2,1)} %collective-permute-done.4), channel_id=1, source_target_pairs={{0,4},{4,8},{8,12},{12,16},{16,20},{20,24},{24,28},{28,0},{1,5},{5... | collective-permute-start | bytes 1179656 | tf_op jit(solution)/shard_map/ppermute | solution.py:17
  66.7 3.7 %copy-start.9 = (bf16[512,4224]{1,0:T(8,128)(2,1)S(1)}, bf16[512,4224]{1,0:T(8,128)(2,1)}, u32[]{:S(2)}) copy-start(bf16[512,4224]{1,0:T(8,128)(2,1)} %all-gather.3.cloned.1.call-done) | copy-start | bytes 12976132
  79.1 0.7 copy-start.10
  79.1 1.0 copy-start.8
  79.1 2.2 copy-start.3
  79.2 7.5 %copy-start.4 = (bf16[16,2048]{1,0:T(8,128)(2,1)S(1)}, bf16[16,2048]{1,0:T(8,128)(2,1)}, u32[]{:S(2)}) copy-start(bf16[16,2048]{1,0:T(8,128)(2,1)} %param.9) | copy-start | bytes 196612
  79.2 154.3 %all-gather.5.cloned.1.call-start = ((), (), s32[]{:S(2)}) async-start(), calls=%async_computation.4 | async-start | bytes 10813440 | tf_op jit(solution)/shard_map/all_gather | solution.py:118
  80.1 0.6 copy-start.6
  83.1 28.7 %copy-start.7 = (f32[16,2]{0,1:T(2,128)S(1)}, f32[16,2]{0,1:T(2,128)}, u32[]{:S(2)}) copy-start(f32[16,2]{0,1:T(2,128)} %copy-done.6) | copy-start | bytes 388
  297.1 5.2 %copy-start = (bf16[1280,2048]{1,0:T(8,128)(2,1)S(1)}, bf16[1280,2048]{1,0:T(8,128)(2,1)}, u32[]{:S(2)}) copy-start(bf16[1280,2048]{1,0:T(8,128)(2,1)} %reshape_squeeze.6) | copy-start | bytes 15728644
  315.0 4.2 %copy-start.11 = (f32[1280,256]{1,0:T(8,128)S(1)}, f32[1280,256]{1,0:T(8,128)}, u32[]{:S(2)}) copy-start(f32[1280,256]{1,0:T(8,128)} %fusion.21) | copy-start | bytes 3932164
  315.0 4.2 %copy-start.12 = (f32[1280,256]{1,0:T(8,128)S(1)}, f32[1280,256]{1,0:T(8,128)}, u32[]{:S(2)}) copy-start(f32[1280,256]{1,0:T(8,128)} %fusion.24) | copy-start | bytes 3932164
  315.0 9.6 %slice-start = ((s8[5242880]{0:T(1024)(128)(4,1)}), s8[4194304]{0:T(1024)(128)(4,1)S(1)}, s32[]{:S(2)}) async-start(s8[5242880]{0:T(1024)(128)(4,1)} %bitcast.16), calls=%async_computation.5 | async-start | bytes 8388608
  319.2 5.4 %slice-start.1 = ((s8[5242880]{0:T(1024)(128)(4,1)}), s8[1048576]{0:T(1024)(128)(4,1)S(1)}, s32[]{:S(2)}) async-start(s8[5242880]{0:T(1024)(128)(4,1)} %bitcast.16), calls=%async_computation.6 | async-start | bytes 2097152
  (1 other events, 0.5 us)
Sparse Core Ops, SparseCore 0:
  11.2 55.5 all-gather.2
  79.3 86.8 reduce-scatter.1
  169.1 64.3 all-gather.4
